TPU v7x, 256 devices: a whole 4x4x8 slice. The times are simulated.
256 devices in a mesh: req: 64 (over z, x, core), tp: 4 (over y).
Axes of the slice: x: 4, y: 4, z: 8, core: 2. Of those that a mesh axis runs over, the one named last changes fastest.
Arguments:
- layer_in: bfloat16 [8192, 2880], P('req', 'tp'), may hold values from -6 to 6
- queries: bfloat16 [8192, 4096], P('req', 'tp'), may hold values from -32 to 32
- key_values: bfloat16 [8192, 2, 512], P('req', None, 'tp'), may hold values from -12 to 12
- prefix_cache: bfloat16 [4, 1024, 2, 512], P(None, 'req', None, 'tp'), may hold values from -8 to 8
- sink_logits: float32 [64], P('tp'), may hold values from 8 to 12
- lengths: int32 [512], P('req'), may hold values from 1 to 16
- groups: int32 [512], P('req'), may hold values from 0 to 3
- batch_home: int32 [64], replicated, may hold values from 0 to 63, each once
- expert_ids: int32 [8192, 4], P('req'), may hold values from 0 to 31, all different within a row; in each aligned block of 128 rows (0 to 127, 128 to 255, ...) at most 24 rows name the same one
- router_logits: float32 [8192, 4], P('req'), may hold values from -6 to 6
- norm_gain: float32 [2880], replicated, may hold values from 0.1 to 1.9
- output_weight: bfloat16 [4096, 2880], P('tp'), may hold values from -0.09375 to 0.09375
- gate_up: bfloat16 [64, 2880, 2, 1440], P('req', None, None, 'tp'), may hold values from -0.109375 to 0.109375
- expert_down: bfloat16 [64, 1440, 2880], P('req', 'tp'), may hold values from -0.109375 to 0.109375
Outputs:
- layer_out: bfloat16 [8192, 2880], P('req', 'tp')
Inputs may be any that keep to these rules, and one draw needn't show every extreme that they name: `expert_ids`: in the token slots of one index of req, no expert is named by more than 24 slots. `batch_home`: A permutation.
All inputs are finite; a program needn't handle non-finite values.
Results may differ from a plain program's by a relative error of at most 0.017.
Values may be sent and summed in bfloat16 or wider, within the bound.
No kernel may reach another device: no remote copies, remote signals or barrier semaphores. Data moves between devices by JAX's collectives and lax.ppermute only.
A program may use at most 192 MiB of HBM per device.

v0:
```python
import jax
import jax.numpy as jnp
from jax import lax
from jax.sharding import PartitionSpec as P

D = 2880
HD = 64
EXPERTS = 32
TOPK = 4
PREFIX = 1024
CAP = 24
theta_base = 150000.0
norm_eps = 1e-05
logit_scale = 0.125
masked_score = -1e30


def rotate(values, positions):
    middle = values.shape[-1] // 2
    lane_index = jnp.arange(middle, dtype=jnp.int32).astype(jnp.float32)
    inverse_freq = theta_base ** (-2.0 * lane_index / values.shape[-1])
    angles = positions.astype(jnp.float32)[:, None] * inverse_freq[None, :]
    cosine = jnp.cos(angles)[:, None, :]
    sine_part = jnp.sin(angles)[:, None, :]
    front_half = values[..., :middle]
    back_half = values[..., middle:]
    return jnp.concatenate(
        [front_half * cosine - back_half * sine_part, back_half * cosine + front_half * sine_part],
        axis=-1,
    )


def absorb_block(softmax_state, query_groups, block_keys, block_values, allowed):
    run_max, run_sum, run_acc = softmax_state
    score_matrix = (
        jnp.einsum(
            "rskgd,rbkd->rskgb", query_groups, block_keys, preferred_element_type=jnp.float32
        )
        * logit_scale
    )
    if allowed is not None:
        score_matrix = jnp.where(allowed, score_matrix, masked_score)
    new_max = jnp.maximum(run_max, jnp.max(score_matrix, axis=-1))
    rescale = jnp.exp(run_max - new_max)
    weights = jnp.exp(score_matrix - new_max[..., None])
    new_sum = run_sum * rescale + jnp.sum(weights, axis=-1)
    new_acc = run_acc * rescale[..., None] + jnp.einsum(
        "rskgb,rbkd->rskgd",
        weights.astype(jnp.bfloat16),
        block_values,
        preferred_element_type=jnp.float32,
    )
    return (new_max, new_sum, new_acc)


def body(
    layer_in,
    queries,
    key_values,
    prefix_cache,
    sink_logits,
    lengths,
    groups,
    batch_home,
    expert_ids,
    router_logits,
    norm_gain,
    output_weight,
    gate_up,
    expert_down,
):
    tokens = queries.shape[0]
    requests = lengths.shape[0]
    suffix = tokens // requests
    local_heads = sink_logits.shape[0]
    kv_local = key_values.shape[2] // HD
    per_group = local_heads // kv_local
    slot_index = jnp.tile(jnp.arange(suffix, dtype=jnp.int32), requests)
    positions = PREFIX + slot_index
    rotated_queries = rotate(
        queries.reshape(tokens, local_heads, HD).astype(jnp.float32), positions
    ).astype(jnp.bfloat16)
    query_groups = rotated_queries.reshape(requests, suffix, kv_local, per_group, HD)
    fresh_keys = rotate(
        key_values[:, 0].reshape(tokens, kv_local, HD).astype(jnp.float32), positions
    ).astype(jnp.bfloat16)
    fresh_keys = fresh_keys.reshape(requests, suffix, kv_local, HD)
    fresh_values = key_values[:, 1].reshape(requests, suffix, kv_local, HD)
    sink_values = sink_logits.reshape(kv_local, per_group)
    state_shape = (requests, suffix, kv_local, per_group)
    start_state = (
        jnp.broadcast_to(sink_values[None, None], state_shape),
        jnp.ones(state_shape, jnp.float32),
        jnp.zeros(state_shape + (HD,), jnp.float32),
    )
    page_rows = lax.all_gather(prefix_cache, "req", axis=1, tiled=True)
    span_rows = page_rows.shape[1]
    block_rows = 512
    chosen = page_rows[groups]
    stacked = chosen.reshape(requests, span_rows // block_rows, block_rows, 2, kv_local, HD)

    def absorb_one(inner_state, block_index):
        block_pair = lax.dynamic_index_in_dim(stacked, block_index, 1, keepdims=False)
        return (
            absorb_block(inner_state, query_groups, block_pair[:, :, 0], block_pair[:, :, 1], None),
            None,
        )

    final_state, _ = lax.scan(absorb_one, start_state, jnp.arange(span_rows // block_rows))
    local_pos = jnp.arange(suffix, dtype=jnp.int32)
    causal = local_pos[None, :] <= local_pos[:, None]
    within = local_pos[None, None, :] < lengths[:, None, None]
    allowed = (causal[None] & within)[:, :, None, None, :]
    run_max, run_sum, run_acc = absorb_block(
        final_state, query_groups, fresh_keys, fresh_values, allowed
    )
    attention = (
        (run_acc / run_sum[..., None]).reshape(tokens, local_heads * HD).astype(jnp.bfloat16)
    )
    partial_value = jnp.dot(attention, output_weight, preferred_element_type=jnp.float32)
    tp_index = lax.axis_index("tp")
    quarter_cols = D // lax.axis_size("tp")
    placed = lax.dynamic_update_slice_in_dim(
        jnp.zeros((tokens, D), jnp.float32),
        layer_in.astype(jnp.float32),
        tp_index * quarter_cols,
        1,
    )
    residual = lax.psum((partial_value + placed).astype(jnp.bfloat16), "tp")
    live_rows = slot_index < jnp.repeat(lengths, suffix)
    pair_weight = jnp.where(live_rows[:, None], jax.nn.softmax(router_logits, axis=-1), 0.0).astype(
        jnp.bfloat16
    )
    flat_ids = expert_ids.reshape(-1)
    onehot = (flat_ids[:, None] == jnp.arange(EXPERTS, dtype=jnp.int32)[None, :]).astype(jnp.int32)
    before = jnp.cumsum(onehot, axis=0) - onehot
    rank_in = jnp.sum(before * onehot, axis=1)
    flat_slot = flat_ids * CAP + rank_in
    pair_token = jnp.arange(tokens * TOPK, dtype=jnp.int32) // TOPK
    token_table = (
        jnp.full((EXPERTS * CAP,), tokens, dtype=jnp.int32)
        .at[flat_slot]
        .set(pair_token)
        .reshape(EXPERTS, CAP)
    )
    weight_table = (
        jnp.zeros((EXPERTS * CAP,), jnp.bfloat16)
        .at[flat_slot]
        .set(pair_weight.reshape(-1))
        .reshape(EXPERTS, CAP)
    )
    devices_req = lax.axis_size("req")
    slab_count = gate_up.shape[0]
    split_count = devices_req * slab_count // EXPERTS
    slab_ids = jnp.arange(devices_req * slab_count, dtype=jnp.int32).reshape(
        devices_req, slab_count
    )
    expert_of = slab_ids // split_count
    token_send = token_table[expert_of]
    weight_send = weight_table[expert_of]
    padded = jnp.concatenate([residual, jnp.zeros((1, residual.shape[1]), jnp.bfloat16)], axis=0)
    rows_send = padded[token_send]
    device_range = jnp.arange(devices_req, dtype=jnp.int32)
    inverse = jnp.sum(
        device_range[:, None] * (batch_home[:, None] == device_range[None, :]).astype(jnp.int32),
        axis=0,
    )
    first_copy = (
        (lax.axis_index("req") * slab_count + jnp.arange(slab_count, dtype=jnp.int32)) % split_count
        == 0
    ).astype(jnp.float32)
    rows_in = lax.all_to_all(rows_send, "req", split_axis=0, concat_axis=0, tiled=True)
    arrived_weight = lax.all_to_all(weight_send, "req", split_axis=0, concat_axis=0, tiled=True)
    arrived_token = lax.all_to_all(token_send, "req", split_axis=0, concat_axis=0, tiled=True)
    rows_float = rows_in.astype(jnp.float32)
    row_scale = lax.rsqrt(jnp.mean(rows_float * rows_float, axis=-1, keepdims=True) + norm_eps)
    normed = (rows_float * row_scale * norm_gain).astype(jnp.bfloat16)
    gate_and_up = jnp.einsum(
        "njcd,jdgf->njcgf", normed, gate_up, preferred_element_type=jnp.float32
    )
    hidden = (jax.nn.silu(gate_and_up[..., 0, :]) * gate_and_up[..., 1, :]).astype(jnp.bfloat16)
    partial_out = jnp.einsum(
        "njcf,jfd->njcd", hidden, expert_down, preferred_element_type=jnp.float32
    )
    value_total = lax.psum_scatter(
        partial_out.astype(jnp.bfloat16), "tp", scatter_dimension=3, tiled=True
    ).astype(jnp.float32)
    own_rows = lax.dynamic_slice_in_dim(rows_float, tp_index * quarter_cols, quarter_cols, 3)
    result = (
        arrived_weight.astype(jnp.float32)[..., None]
        * (value_total + first_copy[None, :, None, None] * own_rows)
    ).astype(jnp.bfloat16)
    moved = result[inverse]
    moved_token = arrived_token[inverse]
    returned = lax.all_to_all(moved, "req", split_axis=0, concat_axis=0, tiled=True)
    returned_token = lax.all_to_all(moved_token, "req", split_axis=0, concat_axis=0, tiled=True)
    flat_rows = returned.reshape(-1, quarter_cols)
    flat_token = returned_token.reshape(-1)
    selector = (jnp.arange(tokens, dtype=jnp.int32)[:, None] == flat_token[None, :]).astype(
        jnp.bfloat16
    )
    return jnp.dot(selector, flat_rows, preferred_element_type=jnp.float32).astype(jnp.bfloat16)


def solution(mesh):
    placed = (
        P("req", "tp"),
        P("req", "tp"),
        P("req", None, "tp"),
        P(None, "req", None, "tp"),
        P("tp"),
        P("req"),
        P("req"),
        P(),
        P("req", None),
        P("req", None),
        P(),
        P("tp", None),
        P("req", None, None, "tp"),
        P("req", "tp", None),
    )
    return jax.shard_map(
        body, mesh=mesh, in_specs=placed, out_specs=P("req", "tp"), check_vma=False
    )
```

profile of v0, /device:TPU:2, one launch (start us, length us, event | category | flops | bytes accessed | tf_op | source)
XLA Modules:
  0.0 776.3 jit_solution(6258052218255485450)
XLA Ops:
  26.4 2.4 fusion.60
  28.8 56.3 %all-gather.2.cloned.1.call-done = bf16[4,1024,2,128]{3,2,1,0:T(2,128)(2,1)} async-done(((bf16[4,16,2,128]{3,2,1,0:T(2,128)(2,1)}), bf16[4,1024,2,128]{3,2,1,0:T(2,128)(2,1)}) %all-gather.2.cloned.1.call-update) | async-done | bytes 2097168 | tf_op jit(solution)/shard_map/all_gather | solution.py:96
  85.1 11.4 %gather_fusion.3 = bf16[8,1024,2,128]{3,2,1,0:T(2,128)(2,1)} fusion(bf16[4,1024,2,128]{3,2,1,0:T(2,128)(2,1)} %all-gather.2.cloned.1.call-done, s32[1024]{0:T(1024)S(1)} %pad_clamp_fusion.1), kind=kCustom, calls=%fused_computation.3 | custom fusion | bytes 8388640 | tf_op jit(solution)/shard_map/gather | solution.py:99
  96.5 17.5 %reshape.462 = bf16[8,2,512,2,2,64]{5,4,3,2,1,0:T(2,128)(2,1)} reshape(bf16[8,1024,2,128]{3,2,1,0:T(2,128)(2,1)} %gather_fusion.3) | data formatting | bytes 8388608 | tf_op jit(solution)/shard_map/reshape | solution.py:100
  114.0 20.0 %copy.79 = bf16[8,2,512,2,2,64]{2,5,4,0,3,1:T(8,128)(2,1)} copy(bf16[8,2,512,2,2,64]{5,4,3,2,1,0:T(2,128)(2,1)} %reshape.462) | data formatting | bytes 8388608
  134.1 26.8 %while.15 = (s32[]{:T(128)}, f32[8,16,2,8]{1,3,2,0:T(8,128)S(1)}, f32[8,16,2,8]{1,3,2,0:T(8,128)S(1)}, f32[8,16,2,8,64]{4,1,3,2,0:T(8,128)S(1)}, s32[2]{0:T(128)...) while((s32[]{:T(128)}, f32[8,16,2,8]{1,3,2,0:T(8,128)S(1)}, ...), condition=%wide.region_11.12_spmd.clone, body=%wide.region_8.11_spmd.clone.sunk | while | flops 277223424 | bytes 46792948 | solution.py:109
  144.1 3.4 fusion.76
  157.4 3.4 fusion.76
  165.1 4.4 fusion.61
  170.6 2.6 scatter_custom_fusion
  175.4 43.8 %all-reduce.3.cloned.1.call-done = bf16[128,2880]{0,1:T(8,128)(2,1)} async-done(((bf16[128,2880]{0,1:T(8,128)(2,1)}), bf16[128,2880]{0,1:T(8,128)(2,1)}) %all-reduce.3.cloned.1.call-update) | async-done | bytes 737296 | tf_op jit(solution)/shard_map/psum | solution.py:129
  222.7 8.1 %gather_fusion.4 = bf16[1536,2880]{1,0:T(8,128)(2,1)} fusion(bf16[129,2880]{1,0:T(8,128)(2,1)S(1)} %concatenate.27.clone, s32[2048]{0:T(1024)S(1)} %pad_clamp_fusion), kind=kCustom, calls=%fused_computation.4 | custom fusion | bytes 17700864 | tf_op jit(solution)/shard_map/gather | solution.py:162
  230.8 210.6 %all_to_all.25 = bf16[64,1,24,2880]{3,2,1,0:T(8,128)(2,1)S(1)} all-to-all(bf16[64,1,24,2880]{3,2,1,0:T(8,128)(2,1)} %bitcast.180), channel_id=1, replica_groups=mesh['req'=64,'tp'=4] {'req'}, dimensions={0} | all-to-all | bytes 17694720 | tf_op jit(solution)/shard_map/all_to_all | solution.py:172
  444.9 10.1 %fusion.25 = f32[64,1,24,2,360]{4,2,3,0,1:T(8,128)S(1)} fusion(bf16[1,2880,2,360]{1,3,2,0:T(8,128)(2,1)} %param.28, f32[2880]{0:T(1024)S(1)} %copy-done.12, f32[64,24]{1,0:T(8,128)S(1)} %add_rsqrt_fusion, bf16[64,1,24,2880]{3,2,1,0:T(8,128)(2,1)S(1)} %all_to_all.25), kind=kOutput, calls=%fused_computation.40 | convolution fusion | flops 6387793920 | bytes 17435904 | tf_op jit(solution)/shard_map/njcd,jdgf->njcgf/dot_general | solution.py:178
  455.1 7.7 convert_bitcast_fusion
  462.8 42.9 %copy.105 = bf16[64,1,24,2880]{2,0,1,3:T(8,128)(2,1)} copy(bf16[64,1,24,2880]{3,2,0,1:T(8,128)(2,1)} %convert_bitcast_fusion) | data formatting | bytes 17694720
  505.7 64.7 %reshape.463 = bf16[2880,1536]{1,0:T(8,128)(2,1)} reshape(bf16[2880,1,64,24]{3,2,1,0:T(8,128)(2,1)} %bitcast.178) | data formatting | bytes 17694720
  571.4 3.8 scatter_custom_fusion.1
  576.6 5.8 all-to-all-start.2
  582.5 8.5 %all-to-all-done.2 = bf16[64,1,24]{2,1,0:T(2,128)(2,1)S(1)} async-done(((bf16[64,1,24]{2,1,0:T(2,128)(2,1)}), bf16[64,1,24]{2,1,0:T(2,128)(2,1)S(1)}, u32[]{:S(2)}, u32[]{:S(2)}) %all-to-all-start.2) | async-done | bytes 3104 | tf_op jit(solution)/shard_map/all_to_all | solution.py:173
  591.0 5.5 all-to-all-start
  596.6 8.6 %all-to-all-done = s32[64,1,24]{2,1,0:T(1,128)S(1)} async-done(((s32[64,1,24]{2,1,0:T(1,128)}), s32[64,1,24]{2,1,0:T(1,128)S(1)}, u32[]{:S(2)}, u32[]{:S(2)}) %all-to-all-start) | async-done | bytes 6176 | tf_op jit(solution)/shard_map/all_to_all | solution.py:174
  606.4 5.9 all-to-all-start.1
  612.2 11.4 %convert_element_type.160 = f32[64,1,24,2880]{3,2,1,0:T(8,128)} convert(bf16[64,1,24,2880]{3,2,1,0:T(8,128)(2,1)} %copy-done.3) | non-fusion elementwise | flops 4423680 | bytes 26542080 | tf_op jit(solution)/shard_map/convert_element_type | solution.py:175
  623.7 29.6 %reduce-scatter.4.cloned.1.call-done = bf16[720,1536]{1,0:T(8,128)(2,1)} async-done(((bf16[2880,1536]{1,0:T(8,128)(2,1)}), bf16[720,1536]{1,0:T(8,128)(2,1)}) %reduce-scatter.4.cloned.1.call-update) | async-done | bytes 2211856
  653.3 21.0 %reshape.464 = bf16[720,1,64,24]{3,2,1,0:T(8,128)(2,1)} reshape(bf16[720,1536]{1,0:T(8,128)(2,1)} %reduce-scatter.4.cloned.1.call-done) | data formatting | bytes 4423680
  674.3 14.0 %copy.106 = bf16[64,1,24,720]{3,2,0,1:T(8,128)(2,1)} copy(bf16[64,1,24,720]{2,0,1,3:T(8,128)(2,1)} %bitcast.179) | data formatting | bytes 4423680
  688.2 6.4 fusion.23
  694.6 3.8 gather_fusion.5
  698.4 10.7 %all-to-all-start.4 = ((bf16[64,1,24,720]{3,2,1,0:T(8,128)(2,1)}), bf16[64,1,24,720]{3,2,1,0:T(8,128)(2,1)}, u32[]{:S(2)}, u32[]{:S(2)}) async-start(bf16[64,1,24,720]{3,2,1,0:T(8,128)(2,1)} %bitcast.181), calls=%async_computation.4 | async-start | bytes 4718592 | tf_op jit(solution)/shard_map/all_to_all | solution.py:195
  710.5 55.5 %all-to-all-done.4 = bf16[64,1,24,720]{3,2,1,0:T(8,128)(2,1)} async-done(((bf16[64,1,24,720]{3,2,1,0:T(8,128)(2,1)}), bf16[64,1,24,720]{3,2,1,0:T(8,128)(2,1)}, u32[]{:S(2)}, u32[]{:S(2)}) %all-to-all-start.4) | async-done | bytes 2211872 | tf_op jit(solution)/shard_map/all_to_all | solution.py:195
  765.9 3.4 convolution_convert_fusion
  (140 shorter events, 54.6 us)
Async XLA Ops:
  6.5 448.5 %copy-start = (bf16[1,360,2880]{2,1,0:T(8,128)(2,1)S(1)}, bf16[1,360,2880]{2,1,0:T(8,128)(2,1)}, u32[]{:S(2)}) copy-start(bf16[1,360,2880]{2,1,0:T(8,128)(2,1)} %param.29) | copy-start | bytes 6220804
  6.5 17.1 %copy-start.9 = (s32[128,4]{0,1:T(4,128)S(1)}, s32[128,4]{0,1:T(4,128)}, u32[]{:S(2)}) copy-start(s32[128,4]{0,1:T(4,128)} %param.24) | copy-start | bytes 6148
  6.5 12.9 %copy-start.6 = (bf16[128,2,128]{2,1,0:T(2,128)(2,1)S(1)}, bf16[128,2,128]{2,1,0:T(2,128)(2,1)}, u32[]{:S(2)}) copy-start(bf16[128,2,128]{2,1,0:T(2,128)(2,1)} %param.18) | copy-start | bytes 196612
  6.5 14.1 %copy-start.13 = (f32[16]{0:T(128)S(1)}, f32[16]{0:T(128)}, u32[]{:S(2)}) copy-start(f32[16]{0:T(128)} %param.20) | copy-start | bytes 196
  6.5 17.4 %copy-start.14 = (s32[8]{0:T(128)S(1)}, s32[8]{0:T(128)}, u32[]{:S(2)}) copy-start(s32[8]{0:T(128)} %param.22) | copy-start | bytes 100
  6.5 78.6 %all-gather.2.cloned.1.call-start = ((), (), s32[]{:S(2)}) async-start(), calls=%async_computation.6 | async-start | bytes 2129920 | tf_op jit(solution)/shard_map/all_gather | solution.py:96
  7.3 212.0 %all-reduce.3.cloned.1.call-start = ((), (), s32[]{:S(2)}) async-start(), calls=%async_computation.7 | async-start | bytes 1474560 | tf_op jit(solution)/shard_map/psum | solution.py:129
  8.4 17.1 %copy-start.15 = (s32[8]{0:T(128)S(1)}, s32[8]{0:T(128)}, u32[]{:S(2)}) copy-start(s32[8]{0:T(128)} %param.21) | copy-start | bytes 100
  25.6 0.8 copy-start.4
  25.7 0.6 copy-start.10
  136.9 3.2 copy-start.5
  138.8 1.3 copy-start.2
  140.8 1.9 copy-start.1
  150.3 3.2 copy-start.5
  152.1 1.3 copy-start.2
  154.2 1.9 copy-start.1
  165.1 4.4 copy-start.7
  170.6 482.7 %reduce-scatter.4.cloned.1.call-start = ((), (), s32[]{:S(2)}) async-start(), calls=%async_computation.8 | async-start | bytes 11059200
  441.5 3.4 copy-start.3
  441.5 3.4 copy-start.12
  570.4 0.6 copy-start.11
  570.4 0.7 copy-start.8
  570.4 12.0 %copy-start.16 = (s32[64]{0:T(128)S(1)}, s32[64]{0:T(128)}, u32[]{:S(2)}) copy-start(s32[64]{0:T(128)} %param.23) | copy-start | bytes 772
  576.6 14.4 %all-to-all-start.2 = ((bf16[64,1,24]{2,1,0:T(2,128)(2,1)}), bf16[64,1,24]{2,1,0:T(2,128)(2,1)S(1)}, u32[]{:S(2)}, u32[]{:S(2)}) async-start(bf16[64,1,24]{2,1,0:T(2,128)(2,1)} %copy.72), calls=%async_computation.2 | async-start | bytes 65536 | tf_op jit(solution)/shard_map/all_to_all | solution.py:173
  591.0 14.2 %all-to-all-start = ((s32[64,1,24]{2,1,0:T(1,128)}), s32[64,1,24]{2,1,0:T(1,128)S(1)}, u32[]{:S(2)}, u32[]{:S(2)}) async-start(s32[64,1,24]{2,1,0:T(1,128)} %bitcast.5), calls=%async_computation | async-start | bytes 65536 | tf_op jit(solution)/shard_map/all_to_all | solution.py:174
  606.4 92.1 %all-to-all-start.1 = ((s32[64,1,24]{2,1,0:T(1,128)}), s32[64,1,24]{2,1,0:T(1,128)S(1)}, u32[]{:S(2)}, u32[]{:S(2)}) async-start(s32[64,1,24]{2,1,0:T(1,128)} %bitcast.10), calls=%async_computation.1 | async-start | bytes 65536 | tf_op jit(solution)/shard_map/all_to_all | solution.py:196
  698.4 67.5 %all-to-all-start.4 = ((bf16[64,1,24,720]{3,2,1,0:T(8,128)(2,1)}), bf16[64,1,24,720]{3,2,1,0:T(8,128)(2,1)}, u32[]{:S(2)}, u32[]{:S(2)}) async-start(bf16[64,1,24,720]{3,2,1,0:T(8,128)(2,1)} %bitcast.181), calls=%async_computation.4 | async-start | bytes 4718592 | tf_op jit(solution)/shard_map/all_to_all | solution.py:195
Sparse Core Ops, SparseCore 0:
  10.0 75.0 all-gather.1
  170.7 48.5 all-reduce.2
  570.5 82.6 reduce-scatter.3
where the time goes:
time: 791 us; the launch traced here: 776 us
  local copies, waits for them, and re-layouts  246 us (31%)
  blocking collectives  211 us (27%)
  waiting for transfers between devices  203 us (26%)
  matrix products  38.4 us (5%)
  other arithmetic  31.5 us (4%)
  starting transfers between devices  28 us (4%)
  between operations  14 us (2%)
    all_to_all x1, blocking collectives, body(): lax.all_to_all(rows_send, 'req', split_axis=0, concat_axis=0, tiled=True)  211 us
    unnamed x37, local copies, waits for them, and re-layouts  170 us
    all_gather x1, waiting for transfers between devices, body(): page_rows = lax.all_gather(prefix_cache, 'req', axis=1, tiled=True)  56.3 us
    all_to_all x1, waiting for transfers between devices, body(): lax.all_to_all(moved, 'req', split_axis=0, concat_axis=0, tiled=True)  55.5 us
    psum x1, waiting for transfers between devices, body(): residual = lax.psum((partial_value + placed).astype(jnp.bfloat16), 'tp')  43.8 us
    unnamed x4, waiting for transfers between devices  30.3 us
    reshape x1, local copies, waits for them, and re-layouts, body(): chosen.reshape(requests, span_rows // block_rows, block_rows, 2, kv_local...  17.5 us
  transfers between devices with their start and end apart: 7, of which 6 were waited for; matrix products, arithmetic and copies ran while one was open for 12% of the time, Pallas kernels for 0%

commit v1 on v0

--- a/solution.py
+++ b/solution.py
@@ -93,7 +93,9 @@
         jnp.ones(state_shape, jnp.float32),
         jnp.zeros(state_shape + (HD,), jnp.float32),
     )
-    page_rows = lax.all_gather(prefix_cache, "req", axis=1, tiled=True)
+    page_rows = jnp.concatenate(
+        lax.all_to_all(jnp.stack([prefix_cache] * lax.axis_size("req")), "req", 0, 0), axis=1
+    )
     span_rows = page_rows.shape[1]
     block_rows = 512
     chosen = page_rows[groups]

time: 791 us -> 763 us (0.965)
  waiting for transfers between devices: 203 us -> 173 us
  starting transfers between devices: 28 us -> 40.3 us
    all_gather x1 -> x0, waiting for transfers between devices: 56.3 us -> none  [body(): page_rows = lax.all_gather(prefix_cache, 'req', axis=1, tiled=True)]
    all_to_all x0 -> x1, waiting for transfers between devices: none -> 29.8 us  [body(): lax.all_to_all(jnp.stack([prefix_cache] * lax.axis_size('req')), 'req', 0...]
    all_to_all x0 -> x1, starting transfers between devices: none -> 12.3 us  [body(): lax.all_to_all(jnp.stack([prefix_cache] * lax.axis_size('req')), 'req', 0...]
    unnamed x4 -> x3, waiting for transfers between devices: 30.3 us -> 29.6 us
    unnamed x37 -> x38, local copies, waits for them, and re-layouts: 170 us -> 171 us
where the time goes in v1:
time: 763 us; the launch traced here: 755 us
  local copies, waits for them, and re-layouts  242 us (32%)
  blocking collectives  211 us (28%)
  waiting for transfers between devices  173 us (23%)
  starting transfers between devices  40.3 us (5%)
  matrix products  38.5 us (5%)
  other arithmetic  32 us (4%)
  between operations  14.1 us (2%)
    all_to_all x1, blocking collectives, body(): lax.all_to_all(rows_send, 'req', split_axis=0, concat_axis=0, tiled=True)  211 us
    unnamed x38, local copies, waits for them, and re-layouts  171 us
    all_to_all x1, waiting for transfers between devices, body(): lax.all_to_all(moved, 'req', split_axis=0, concat_axis=0, tiled=True)  55.5 us
    psum x1, waiting for transfers between devices, body(): residual = lax.psum((partial_value + placed).astype(jnp.bfloat16), 'tp')  41.3 us
    all_to_all x1, waiting for transfers between devices, body(): lax.all_to_all(jnp.stack([prefix_cache] * lax.axis_size('req')), 'req', 0...  29.8 us
    unnamed x3, waiting for transfers between devices  29.6 us
  transfers between devices with their start and end apart: 7, of which 6 were waited for; matrix products, arithmetic and copies ran while one was open for 12% of the time, Pallas kernels for 0%

profile of v1, /device:TPU:2, one launch (start us, length us, event | category | flops | bytes accessed | tf_op | source)
XLA Modules:
  0.0 755.2 jit_solution(14975806135813404936)
XLA Ops:
  9.3 12.3 %all-to-all-start.3 = ((bf16[64,4,16,2,128]{4,2,3,1,0:T(8,128)(2,1)}), bf16[64,4,16,2,128]{4,2,3,1,0:T(8,128)(2,1)}, u32[]{:S(2)}, u32[]{:S(2)}) async-start(bf16[64,4,16,2,128]{4,2,3,1,0:T(8,128)(2,1)} %stack.2), calls=%async_computation.3 | async-start | bytes 4194304 | tf_op jit(solution)/shard_map/all_to_all | solution.py:97
  43.0 29.8 %all-to-all-done.3 = bf16[64,4,16,2,128]{4,2,3,1,0:T(8,128)(2,1)} async-done(((bf16[64,4,16,2,128]{4,2,3,1,0:T(8,128)(2,1)}), bf16[64,4,16,2,128]{4,2,3,1,0:T(8,128)(2,1)}, u32[]{:S(2)}, u32[]{:S(2)}) %all-to-all-start.3) | async-done | bytes 2097184 | tf_op jit(solution)/shard_map/all_to_all | solution.py:97
  72.8 3.3 copy.77
  76.0 4.6 gather_fusion.3
  80.7 14.7 %reshape.472 = bf16[8,2,512,2,2,64]{5,4,2,1,3,0:T(2,128)(2,1)} reshape(bf16[8,1024,2,128]{3,1,2,0:T(8,128)(2,1)} %gather_fusion.3) | data formatting | bytes 8388608 | tf_op jit(solution)/shard_map/reshape | solution.py:102
  95.4 20.0 %copy.84 = bf16[8,2,512,2,2,64]{2,5,4,0,3,1:T(8,128)(2,1)} copy(bf16[8,2,512,2,2,64]{5,4,2,1,3,0:T(2,128)(2,1)} %reshape.472) | data formatting | bytes 8388608
  115.5 26.8 %while.15 = (s32[]{:T(128)}, f32[8,16,2,8]{1,3,2,0:T(8,128)S(1)}, f32[8,16,2,8]{1,3,2,0:T(8,128)S(1)}, f32[8,16,2,8,64]{4,1,3,2,0:T(8,128)S(1)}, s32[2]{0:T(128)...) while((s32[]{:T(128)}, f32[8,16,2,8]{1,3,2,0:T(8,128)S(1)}, ...), condition=%wide.region_11.12_spmd.clone, body=%wide.region_8.11_spmd.clone.sunk | while | flops 277223424 | bytes 46792948 | solution.py:111
  125.4 3.4 fusion.76
  138.8 3.4 fusion.76
  146.5 4.4 fusion.61
  156.6 41.3 %all-reduce.3.cloned.1.call-done = bf16[128,2880]{0,1:T(8,128)(2,1)} async-done(((bf16[128,2880]{0,1:T(8,128)(2,1)}), bf16[128,2880]{0,1:T(8,128)(2,1)}) %all-reduce.3.cloned.1.call-update) | async-done | bytes 737296 | tf_op jit(solution)/shard_map/psum | solution.py:131
  201.3 8.1 %gather_fusion.4 = bf16[1536,2880]{1,0:T(8,128)(2,1)} fusion(bf16[129,2880]{1,0:T(8,128)(2,1)S(1)} %concatenate.27.clone, s32[2048]{0:T(1024)S(1)} %pad_clamp_fusion), kind=kCustom, calls=%fused_computation.4 | custom fusion | bytes 17700864 | tf_op jit(solution)/shard_map/gather | solution.py:164
  209.5 210.8 %all_to_all.30 = bf16[64,1,24,2880]{3,2,1,0:T(8,128)(2,1)S(1)} all-to-all(bf16[64,1,24,2880]{3,2,1,0:T(8,128)(2,1)} %bitcast.187), channel_id=1, replica_groups=mesh['req'=64,'tp'=4] {'req'}, dimensions={0} | all-to-all | bytes 17694720 | tf_op jit(solution)/shard_map/all_to_all | solution.py:174
  423.7 10.1 %fusion.25 = f32[64,1,24,2,360]{4,2,3,0,1:T(8,128)S(1)} fusion(bf16[1,2880,2,360]{1,3,2,0:T(8,128)(2,1)} %param.28, f32[2880]{0:T(1024)S(1)} %copy-done.12, f32[64,24]{1,0:T(8,128)S(1)} %add_rsqrt_fusion, bf16[64,1,24,2880]{3,2,1,0:T(8,128)(2,1)S(1)} %all_to_all.30), kind=kOutput, calls=%fused_computation.40 | convolution fusion | flops 6387793920 | bytes 17435904 | tf_op jit(solution)/shard_map/njcd,jdgf->njcgf/dot_general | solution.py:180
  433.9 7.7 %convert_bitcast_fusion = bf16[64,1,24,2880]{3,2,0,1:T(8,128)(2,1)} fusion(bf16[1,360,2880]{2,1,0:T(8,128)(2,1)S(1)} %copy-done, f32[64,1,24,2,360]{4,2,3,0,1:T(8,128)S(1)} %fusion.25), kind=kOutput, calls=%fused_computation.31 | convolution fusion | flops 3192791040 | bytes 15344640 | tf_op jit(solution)/shard_map/njcf,jfd->njcd/dot_general | solution.py:184
  441.6 42.9 %copy.110 = bf16[64,1,24,2880]{2,0,1,3:T(8,128)(2,1)} copy(bf16[64,1,24,2880]{3,2,0,1:T(8,128)(2,1)} %convert_bitcast_fusion) | data formatting | bytes 17694720
  484.5 64.7 %reshape.473 = bf16[2880,1536]{1,0:T(8,128)(2,1)} reshape(bf16[2880,1,64,24]{3,2,1,0:T(8,128)(2,1)} %bitcast.185) | data formatting | bytes 17694720
  550.3 3.8 scatter_custom_fusion.1
  555.4 5.8 all-to-all-start.2
  561.3 8.5 %all-to-all-done.2 = bf16[64,1,24]{2,1,0:T(2,128)(2,1)S(1)} async-done(((bf16[64,1,24]{2,1,0:T(2,128)(2,1)}), bf16[64,1,24]{2,1,0:T(2,128)(2,1)S(1)}, u32[]{:S(2)}, u32[]{:S(2)}) %all-to-all-start.2) | async-done | bytes 3104 | tf_op jit(solution)/shard_map/all_to_all | solution.py:175
  569.8 5.5 all-to-all-start
  575.4 8.6 %all-to-all-done = s32[64,1,24]{2,1,0:T(1,128)S(1)} async-done(((s32[64,1,24]{2,1,0:T(1,128)}), s32[64,1,24]{2,1,0:T(1,128)S(1)}, u32[]{:S(2)}, u32[]{:S(2)}) %all-to-all-start) | async-done | bytes 6176 | tf_op jit(solution)/shard_map/all_to_all | solution.py:176
  585.2 5.9 all-to-all-start.1
  591.1 11.4 %convert_element_type.160 = f32[64,1,24,2880]{3,2,1,0:T(8,128)} convert(bf16[64,1,24,2880]{3,2,1,0:T(8,128)(2,1)} %copy-done.3) | non-fusion elementwise | flops 4423680 | bytes 26542080 | tf_op jit(solution)/shard_map/convert_element_type | solution.py:177
  602.5 29.6 %reduce-scatter.4.cloned.1.call-done = bf16[720,1536]{1,0:T(8,128)(2,1)} async-done(((bf16[2880,1536]{1,0:T(8,128)(2,1)}), bf16[720,1536]{1,0:T(8,128)(2,1)}) %reduce-scatter.4.cloned.1.call-update) | async-done | bytes 2211856
  632.1 21.0 %reshape.474 = bf16[720,1,64,24]{3,2,1,0:T(8,128)(2,1)} reshape(bf16[720,1536]{1,0:T(8,128)(2,1)} %reduce-scatter.4.cloned.1.call-done) | data formatting | bytes 4423680
  653.1 14.0 %copy.111 = bf16[64,1,24,720]{3,2,0,1:T(8,128)(2,1)} copy(bf16[64,1,24,720]{2,0,1,3:T(8,128)(2,1)} %bitcast.186) | data formatting | bytes 4423680
  667.1 6.4 fusion.23
  673.5 3.8 gather_fusion.5
  677.2 10.7 %all-to-all-start.5 = ((bf16[64,1,24,720]{3,2,1,0:T(8,128)(2,1)}), bf16[64,1,24,720]{3,2,1,0:T(8,128)(2,1)}, u32[]{:S(2)}, u32[]{:S(2)}) async-start(bf16[64,1,24,720]{3,2,1,0:T(8,128)(2,1)} %bitcast.189), calls=%async_computation.5 | async-start | bytes 4718592 | tf_op jit(solution)/shard_map/all_to_all | solution.py:197
  689.3 55.5 %all-to-all-done.5 = bf16[64,1,24,720]{3,2,1,0:T(8,128)(2,1)} async-done(((bf16[64,1,24,720]{3,2,1,0:T(8,128)(2,1)}), bf16[64,1,24,720]{3,2,1,0:T(8,128)(2,1)}, u32[]{:S(2)}, u32[]{:S(2)}) %all-to-all-start.5) | async-done | bytes 2211872 | tf_op jit(solution)/shard_map/all_to_all | solution.py:197
  744.7 3.4 convolution_convert_fusion
  (142 shorter events, 61.4 us)
Async XLA Ops:
  6.5 427.4 %copy-start = (bf16[1,360,2880]{2,1,0:T(8,128)(2,1)S(1)}, bf16[1,360,2880]{2,1,0:T(8,128)(2,1)}, u32[]{:S(2)}) copy-start(bf16[1,360,2880]{2,1,0:T(8,128)(2,1)} %param.29) | copy-start | bytes 6220804
  6.5 15.2 %copy-start.9 = (s32[128,4]{0,1:T(4,128)S(1)}, s32[128,4]{0,1:T(4,128)}, u32[]{:S(2)}) copy-start(s32[128,4]{0,1:T(4,128)} %param.24) | copy-start | bytes 6148
  9.3 23.8 %copy-start.6 = (bf16[128,2,128]{2,1,0:T(2,128)(2,1)S(1)}, bf16[128,2,128]{2,1,0:T(2,128)(2,1)}, u32[]{:S(2)}) copy-start(bf16[128,2,128]{2,1,0:T(2,128)(2,1)} %param.18) | copy-start | bytes 196612
  9.3 63.5 %all-to-all-start.3 = ((bf16[64,4,16,2,128]{4,2,3,1,0:T(8,128)(2,1)}), bf16[64,4,16,2,128]{4,2,3,1,0:T(8,128)(2,1)}, u32[]{:S(2)}, u32[]{:S(2)}) async-start(bf16[64,4,16,2,128]{4,2,3,1,0:T(8,128)(2,1)} %stack.2), calls=%async_computation.3 | async-start | bytes 4194304 | tf_op jit(solution)/shard_map/all_to_all | solution.py:97
  21.6 12.7 %copy-start.13 = (f32[16]{0:T(128)S(1)}, f32[16]{0:T(128)}, u32[]{:S(2)}) copy-start(f32[16]{0:T(128)} %param.20) | copy-start | bytes 196
  21.6 16.5 %copy-start.14 = (s32[8]{0:T(128)S(1)}, s32[8]{0:T(128)}, u32[]{:S(2)}) copy-start(s32[8]{0:T(128)} %param.22) | copy-start | bytes 100
  21.6 176.3 %all-reduce.3.cloned.1.call-start = ((), (), s32[]{:S(2)}) async-start(), calls=%async_computation.7 | async-start | bytes 1474560 | tf_op jit(solution)/shard_map/psum | solution.py:131
  22.1 17.6 %copy-start.15 = (s32[8]{0:T(128)S(1)}, s32[8]{0:T(128)}, u32[]{:S(2)}) copy-start(s32[8]{0:T(128)} %param.21) | copy-start | bytes 100
  39.8 0.8 copy-start.4
  39.9 0.6 copy-start.10
  118.2 3.2 copy-start.5
  120.1 1.3 copy-start.2
  122.2 1.9 copy-start.1
  131.6 3.2 copy-start.5
  133.5 1.3 copy-start.2
  135.6 1.9 copy-start.1
  146.4 4.4 copy-start.7
  151.9 480.2 %reduce-scatter.4.cloned.1.call-start = ((), (), s32[]{:S(2)}) async-start(), calls=%async_computation.8 | async-start | bytes 11059200
  420.3 3.4 copy-start.3
  420.3 3.4 copy-start.12
  549.2 0.6 copy-start.11
  549.2 0.7 copy-start.8
  549.2 12.0 %copy-start.16 = (s32[64]{0:T(128)S(1)}, s32[64]{0:T(128)}, u32[]{:S(2)}) copy-start(s32[64]{0:T(128)} %param.23) | copy-start | bytes 772
  555.4 14.4 %all-to-all-start.2 = ((bf16[64,1,24]{2,1,0:T(2,128)(2,1)}), bf16[64,1,24]{2,1,0:T(2,128)(2,1)S(1)}, u32[]{:S(2)}, u32[]{:S(2)}) async-start(bf16[64,1,24]{2,1,0:T(2,128)(2,1)} %copy.75), calls=%async_computation.2 | async-start | bytes 65536 | tf_op jit(solution)/shard_map/all_to_all | solution.py:175
  569.8 14.2 %all-to-all-start = ((s32[64,1,24]{2,1,0:T(1,128)}), s32[64,1,24]{2,1,0:T(1,128)S(1)}, u32[]{:S(2)}, u32[]{:S(2)}) async-start(s32[64,1,24]{2,1,0:T(1,128)} %bitcast.5), calls=%async_computation | async-start | bytes 65536 | tf_op jit(solution)/shard_map/all_to_all | solution.py:176
  585.2 92.1 %all-to-all-start.1 = ((s32[64,1,24]{2,1,0:T(1,128)}), s32[64,1,24]{2,1,0:T(1,128)S(1)}, u32[]{:S(2)}, u32[]{:S(2)}) async-start(s32[64,1,24]{2,1,0:T(1,128)} %bitcast.10), calls=%async_computation.1 | async-start | bytes 65536 | tf_op jit(solution)/shard_map/all_to_all | solution.py:198
  677.2 67.5 %all-to-all-start.5 = ((bf16[64,1,24,720]{3,2,1,0:T(8,128)(2,1)}), bf16[64,1,24,720]{3,2,1,0:T(8,128)(2,1)}, u32[]{:S(2)}, u32[]{:S(2)}) async-start(bf16[64,1,24,720]{3,2,1,0:T(8,128)(2,1)} %bitcast.189), calls=%async_computation.5 | async-start | bytes 4718592 | tf_op jit(solution)/shard_map/all_to_all | solution.py:197
Sparse Core Ops, SparseCore 0:
  152.0 45.8 all-reduce.2
  549.4 82.6 reduce-scatter.3
